TPU v7x, 32 devices: a whole 2x2x4 slice. The times are simulated.
32 devices in a mesh: dp: 2 (over y), mp: 16 (over z, x, core).
Axes of the slice: x: 2, y: 2, z: 4, core: 2. Of those that a mesh axis runs over, the one named last changes fastest.
Arguments:
- queries: bfloat16 [2048, 1024], P(('dp', 'mp')), may hold values from -16 to 16
- hidden: bfloat16 [2048, 2048], P(('dp', 'mp')), may hold values from -6 to 6
- kv_pages: bfloat16 [192, 16, 2, 1024], P(('dp', 'mp')), may hold values from -8 to 8
- page_table: int32 [2, 96], replicated, may hold values from 0 to 191, as said below
- cache_len: int32 [2], replicated, may hold values from 1 to 512, as said below
- deal_table: int32 [2, 16], P('dp'), may hold values from 0 to 15, as said below
- out_weight: bfloat16 [1024, 2048], P('dp', 'mp'), may hold values from -0.1875 to 0.1875
- norm_gain: float32 [2048], replicated, may hold values from 0.1 to 1.9
- expert_ids: int32 [2048, 6], P(('dp', 'mp')), may hold values from 0 to 15, all different within a row; in each aligned block of 64 rows (0 to 63, 64 to 127, ...) at most 32 rows name the same one
- expert_gates: float32 [2048, 6], P(('dp', 'mp')), may hold values from 0.05 to 0.5
- experts_in: bfloat16 [16, 2048, 1408], P('mp', 'dp'), may hold values from -0.125 to 0.125
- experts_out: bfloat16 [16, 704, 2048], P('mp', None, 'dp'), may hold values from -0.21875 to 0.21875
Outputs:
- mixed: bfloat16 [2048, 2048], P(('dp', 'mp'))
Inputs may be any that keep to these rules, and one draw needn't show every extreme that they name: `deal_table`: each row is an ordering of 0 to 15: every piece of the 1 request of row d is held by one device of that row. For request r = d + j, the entries page_table[r, l] over all l are exactly the pages (d * 16 + m) * 6 + j * 6 + k for m < 16, k < 6, each once, in an order given by the draw. `cache_len`: some request has 512 cached tokens and some has 1. `expert_ids`: the 6 ids of a token differ; among the 64 tokens of one device no expert is named more than 32 times, and in some device one expert is named exactly 32 times.
All inputs are finite; a program needn't handle non-finite values.
Results may differ from a plain program's by a relative error of at most 0.0095.
Values may be sent and summed in bfloat16 or wider, within the bound.
No kernel may reach another device: no remote copies, remote signals or barrier semaphores. Data moves between devices by JAX's collectives and lax.ppermute only.
A program may use at most 128 MiB of HBM per device.

v0:
```python
import math
import jax
import jax.numpy as jnp
from jax import lax
from jax.sharding import PartitionSpec as P

HEADS = 8
HD = 128
TOPK = 6
PAGE = 16
epsilon = 1e-06


def attend_head(q_rows, key_rows, value_rows, key_pos, query_pos):
    scores = jnp.dot(q_rows, key_rows.T, preferred_element_type=jnp.float32) * (1.0 / math.sqrt(HD))
    allowed = key_pos[None, :] <= query_pos[:, None]
    scores = jnp.where(allowed, scores, -1e30)
    row_max = jnp.max(scores, axis=1, keepdims=True)
    weights = jnp.exp(scores - row_max)
    weights_bf = (weights / jnp.sum(weights, axis=1, keepdims=True)).astype(jnp.bfloat16)
    blended = jnp.dot(weights_bf, value_rows, preferred_element_type=jnp.float32)
    return blended.astype(jnp.bfloat16)


def swap_dp(x):
    return lax.ppermute(x, "dp", [(0, 1), (1, 0)])


def on_device(
    queries,
    hidden,
    kv_pages,
    page_table,
    cache_len,
    deal_table,
    out_weight,
    norm_gain,
    expert_ids,
    expert_gates,
    experts_in,
    experts_out,
):
    n_mp = lax.axis_size("mp")
    n_dp = lax.axis_size("dp")
    row_index = lax.axis_index("dp")
    column = lax.axis_index("mp")
    q_count = queries.shape[0]
    width = queries.shape[1]
    d_model = hidden.shape[1]
    heads = width // HD
    groups = n_mp // heads
    sub = q_count // groups
    my_head = column % heads
    my_group = column // heads
    page_share = page_table.shape[1] // n_mp
    pages_dev = kv_pages.shape[0]
    deal_row = deal_table[0]
    request = row_index
    page_count = page_table.shape[1]
    q_out = queries.reshape(sub, groups, heads, HD).transpose(1, 2, 0, 3).reshape(n_mp, sub, HD)
    kv_heads = kv_pages.reshape(pages_dev, PAGE, 2, heads, HD).transpose(3, 0, 1, 2, 4)
    kv_out = jnp.tile(kv_heads, (groups, 1, 1, 1, 1)).reshape(n_mp, pages_dev * PAGE * 2, HD)
    if n_dp == 2:
        w_pair = swap_dp(out_weight)
        wo_rows = jnp.where(
            row_index == 0,
            jnp.concatenate([out_weight, w_pair], axis=0),
            jnp.concatenate([w_pair, out_weight], axis=0),
        )
    else:
        wo_rows = lax.all_gather(out_weight, "dp", axis=0, tiled=True)
    bits = n_mp.bit_length() - 1
    kv_send = jnp.concatenate([q_out, kv_out], axis=1)
    if n_mp == 1 << bits:
        block = wo_rows[None]
        if bits > 2 and n_dp == 2:
            t1, t2 = (bits - 1, bits - 2)
            fetched = {}
            for a in range(2):
                for c in range(2):
                    off = a << t1 | c << t2
                    near = (
                        out_weight
                        if off == 0
                        else lax.ppermute(out_weight, "mp", [(m, m ^ off) for m in range(n_mp)])
                    )
                    other = lax.ppermute(
                        out_weight,
                        ("dp", "mp"),
                        [
                            (d * n_mp + m, (1 - d) * n_mp + (m ^ off))
                            for d in range(2)
                            for m in range(n_mp)
                        ],
                    )
                    fetched[a, c] = jnp.where(
                        row_index == 0,
                        jnp.concatenate([near, other], axis=0),
                        jnp.concatenate([other, near], axis=0),
                    )
            b1 = (column >> t1) % 2
            b2 = (column >> t2) % 2
            shards = []
            for x2 in range(2):
                for x3 in range(2):
                    a0 = b1 ^ x3 == 0
                    c0 = b2 ^ x2 == 0
                    shards.append(
                        jnp.where(
                            a0,
                            jnp.where(c0, fetched[0, 0], fetched[0, 1]),
                            jnp.where(c0, fetched[1, 0], fetched[1, 1]),
                        )
                    )
            block = jnp.stack(shards)
        elif bits > 1:
            b = bits - 1
            pair = lax.ppermute(block, "mp", [(m, m ^ 1 << b) for m in range(n_mp)])
            low = (column >> b) % 2 == 0
            block = jnp.concatenate(
                [jnp.where(low, block, pair), jnp.where(low, pair, block)], axis=0
            )
        block, kv_send = lax.optimization_barrier((block, kv_send))
    both = lax.all_to_all(kv_send, "mp", split_axis=0, concat_axis=0, tiled=True)
    q_in = both[:, :sub, :]
    arrived = both[:, sub:, :].reshape(n_mp, pages_dev, PAGE, 2, HD)
    first_pos = cache_len[request] + deal_row % n_mp * q_count
    query_pos = (
        first_pos[:, None] + jnp.arange(sub, dtype=jnp.int32)[None, :] * groups + my_group
    ).reshape(-1)
    slot_ids = jnp.arange(n_mp * page_share, dtype=jnp.int32)
    physical = (row_index * n_mp + slot_ids // page_share) * pages_dev + slot_ids % page_share
    table_row = page_table[request]
    matches = table_row[None, :] == physical[:, None]
    logical = jnp.sum(
        jnp.where(matches, jnp.arange(page_count, dtype=jnp.int32)[None, :], 0), axis=1
    )
    key_pos = (logical[:, None] * PAGE + jnp.arange(PAGE, dtype=jnp.int32)[None, :]).reshape(-1)
    key_rows = arrived[:, :, :, 0, :].reshape(-1, HD)
    value_rows = arrived[:, :, :, 1, :].reshape(-1, HD)
    blended = attend_head(q_in.reshape(-1, HD), key_rows, value_rows, key_pos, query_pos)
    back = lax.all_to_all(
        blended.reshape(n_mp, sub, HD), "mp", split_axis=0, concat_axis=0, tiled=True
    )
    attended = back.reshape(groups, heads, sub, HD).transpose(2, 0, 1, 3).reshape(q_count, width)
    bits = n_mp.bit_length() - 1
    if n_mp == 1 << bits:
        for b in reversed(range(1, bits - 2 if n_dp == 2 and bits > 2 else bits - 1)):
            pair = lax.ppermute(block, "mp", [(m, m ^ 1 << b) for m in range(n_mp)])
            low = (column >> b) % 2 == 0
            block = jnp.concatenate(
                [jnp.where(low, block, pair), jnp.where(low, pair, block)], axis=0
            )
        pair = lax.ppermute(block, "mp", [(m, m ^ 1) for m in range(n_mp)])
        own_part = jnp.einsum("tk,jkc->tjc", attended, block, preferred_element_type=jnp.float32)
        pair_part = jnp.einsum("tk,jkc->tjc", attended, pair, preferred_element_type=jnp.float32)
        low = column % 2 == 0
        by_shard = jnp.where(
            low,
            jnp.concatenate([own_part, pair_part], axis=1),
            jnp.concatenate([pair_part, own_part], axis=1),
        )
        order = (0,) + tuple(range(bits, 0, -1)) + (bits + 1,)
        shard_w = wo_rows.shape[1]
        projected = (
            by_shard.reshape((q_count,) + (2,) * bits + (shard_w,))
            .transpose(order)
            .reshape(q_count, d_model)
        )
    else:
        projected = jnp.dot(
            attended,
            lax.all_gather(wo_rows, "mp", axis=1, tiled=True),
            preferred_element_type=jnp.float32,
        )
    resid_f = (hidden.astype(jnp.float32) + projected).astype(jnp.bfloat16).astype(jnp.float32)
    mean_square = jnp.mean(resid_f * resid_f, axis=1, keepdims=True)
    normed = (resid_f * lax.rsqrt(mean_square + epsilon) * norm_gain[None, :]).astype(jnp.bfloat16)
    capacity = min(q_count, q_count * TOPK * 4 // (3 * n_mp))
    flat_ids = expert_ids.reshape(-1)
    one_hot = (flat_ids[:, None] == jnp.arange(n_mp, dtype=jnp.int32)[None, :]).astype(jnp.int32)
    slot_of = jnp.sum(jnp.cumsum(one_hot, axis=0) * one_hot, axis=1) - 1
    target = (flat_ids * capacity + slot_of).reshape(q_count, TOPK)
    hits = target[:, :, None] == jnp.arange(n_mp * capacity, dtype=jnp.int32)[None, None, :]
    dispatch = jnp.any(hits, axis=1).astype(jnp.bfloat16)
    combine = jnp.sum(jnp.where(hits, expert_gates[:, :, None], 0.0), axis=1)
    ff_width = experts_out.shape[1]
    if n_dp == 2:
        out_other = swap_dp(experts_out)
        in_other = swap_dp(experts_in)
        normed, out_other = lax.optimization_barrier((normed, out_other))
    sending = lax.dot_general(
        dispatch, normed, (((0,), (0,)), ((), ())), preferred_element_type=jnp.float32
    ).astype(jnp.bfloat16)
    received = lax.all_to_all(
        sending.reshape(n_mp, capacity, d_model), "mp", split_axis=0, concat_axis=0, tiled=True
    )
    flat_rows = received.reshape(-1, d_model)
    if n_dp == 2:
        first = row_index == 0
        gate_up = jnp.where(
            first,
            jnp.concatenate([experts_in[0], in_other[0]], axis=0),
            jnp.concatenate([in_other[0], experts_in[0]], axis=0),
        )
        down = jnp.where(
            first,
            jnp.concatenate([experts_out[0], out_other[0]], axis=1),
            jnp.concatenate([out_other[0], experts_out[0]], axis=1),
        )
        flat_rows, down, gate_up = lax.optimization_barrier((flat_rows, down, gate_up))
    else:
        gate_up = lax.all_gather(experts_in, "dp", axis=1, tiled=True)[0]
        down = lax.all_gather(experts_out, "dp", axis=2, tiled=True)[0]
    gate_vals = jnp.dot(flat_rows, gate_up, preferred_element_type=jnp.float32)
    act = (jax.nn.silu(gate_vals[:, :ff_width]) * gate_vals[:, ff_width:]).astype(jnp.bfloat16)
    outcome = jnp.dot(act, down, preferred_element_type=jnp.float32).astype(jnp.bfloat16)
    results = lax.all_to_all(
        outcome.reshape(n_mp, capacity, d_model), "mp", split_axis=0, concat_axis=0, tiled=True
    )
    expert_sum = jnp.dot(
        combine,
        results.reshape(-1, d_model).astype(jnp.float32),
        precision=lax.Precision.HIGHEST,
        preferred_element_type=jnp.float32,
    )
    return (resid_f + expert_sum).astype(jnp.bfloat16)


def solution(mesh):
    in_specs = (
        P(("dp", "mp"), None),
        P(("dp", "mp"), None),
        P(("dp", "mp"), None, None, None),
        P(),
        P(),
        P("dp", None),
        P("dp", "mp"),
        P(),
        P(("dp", "mp"), None),
        P(("dp", "mp"), None),
        P("mp", "dp", None),
        P("mp", None, "dp"),
    )
    out_specs = P(("dp", "mp"), None)
    return jax.shard_map(
        on_device, mesh=mesh, in_specs=in_specs, out_specs=out_specs, check_vma=False
    )
```

profile of v0, /device:TPU:11, one launch (start us, length us, event | category | flops | bytes accessed | tf_op | source)
XLA Modules:
  0.0 202.7 jit_solution(180145341147619317)
XLA Ops:
  0.0 2.3 %collective-permute-start.6 = (bf16[512,128]{1,0:T(8,128)(2,1)}, bf16[512,128]{1,0:T(8,128)(2,1)S(1)}, u32[]{:S(2)}, u32[]{:S(2)}) collective-permute-start(bf16[512,128]{1,0:T(8,128)(2,1)} %param.18), channel_id=1, source_target_pairs={{0,28},{1,29},{2,30},{3,31},{4,24},{5,25},{6,26},{7,27},{8,20},{9,... | collective-permute-start | bytes 393224 | tf_op jit(solution)/shard_map/ppermute | solution.py:87
  2.3 0.2 collective-permute-start
  2.5 2.2 %collective-permute-start.1 = (bf16[512,128]{1,0:T(8,128)(2,1)}, bf16[512,128]{1,0:T(8,128)(2,1)S(1)}, u32[]{:S(2)}, u32[]{:S(2)}) collective-permute-start(bf16[512,128]{1,0:T(8,128)(2,1)} %param.18), channel_id=1, source_target_pairs={{0,4},{1,5},{2,6},{3,7},{4,0},{5,1},{6,2},{7,3},{8,12},{9,13},{10,... | collective-permute-start | bytes 393224 | tf_op jit(solution)/shard_map/ppermute | solution.py:85
  4.7 1.0 collective-permute-start.2
  5.9 0.8 copy.72
  6.8 0.9 reduce-window.6
  8.1 1.2 reshape.608
  9.4 0.3 copy.66
  9.7 0.9 copy.77
  10.8 2.2 %collective-permute-start.4 = (bf16[512,128]{1,0:T(8,128)(2,1)}, bf16[512,128]{1,0:T(8,128)(2,1)S(1)}, u32[]{:S(2)}, u32[]{:S(2)}) collective-permute-start(bf16[512,128]{1,0:T(8,128)(2,1)} %param.18), channel_id=1, source_target_pairs={{0,24},{1,25},{2,26},{3,27},{4,28},{5,29},{6,30},{7,31},{8,16},{9,... | collective-permute-start | bytes 393224 | tf_op jit(solution)/shard_map/ppermute | solution.py:87
  13.0 0.4 collective-permute-start.5
  13.4 0.6 tile.8
  14.0 1.0 pad_maximum_fusion.2
  15.0 1.1 collective-permute-start.9
  16.1 0.4 collective-permute-start.10
  16.4 7.3 %collective-permute-done.4 = bf16[512,128]{1,0:T(8,128)(2,1)S(1)} collective-permute-done((bf16[512,128]{1,0:T(8,128)(2,1)}, bf16[512,128]{1,0:T(8,128)(2,1)S(1)}, u32[]{:S(2)}, u32[]{:S(2)}) %collective-permute-start.4) | collective-permute-done | bytes 131104 | tf_op jit(solution)/shard_map/ppermute | solution.py:87
  23.8 3.7 %collective-permute-done.5 = bf16[512,128]{1,0:T(8,128)(2,1)S(1)} collective-permute-done((bf16[512,128]{1,0:T(8,128)(2,1)}, bf16[512,128]{1,0:T(8,128)(2,1)S(1)}, u32[]{:S(2)}, u32[]{:S(2)}) %collective-permute-start.5) | collective-permute-done | bytes 131104 | tf_op jit(solution)/shard_map/ppermute | solution.py:85
  27.5 0.3 broadcast_select_fusion.4
  27.7 0.3 broadcast_select_fusion.5
  28.0 0.3 broadcast_select_fusion.8
  28.3 0.3 broadcast_select_fusion.9
  28.8 0.3 collective-permute-start.7
  29.3 0.6 dynamic_slice.7
  29.9 6.0 %all-to-all-start = ((bf16[16,224,128]{2,1,0:T(8,128)(2,1)}), bf16[16,224,128]{2,1,0:T(8,128)(2,1)S(1)}, u32[]{:S(2)}, u32[]{:S(2)}) async-start(bf16[16,224,128]{2,1,0:T(8,128)(2,1)} %pad_maximum_fusion.2), calls=%async_computation | async-start | bytes 1835008 | tf_op jit(solution)/shard_map/all_to_all | solution.py:124
  35.9 0.7 fusion.19
  36.7 23.9 %collective-permute-done.7 = bf16[4,1024,128]{2,1,0:T(8,128)(2,1)S(1)} collective-permute-done((bf16[4,1024,128]{2,1,0:T(8,128)(2,1)S(1)}, bf16[4,1024,128]{2,1,0:T(8,128)(2,1)S(1)}, u32[]{:S(2)}, u32[]{:S(2)}) %collective-permute-start.7) | collective-permute-done | bytes 1048608 | tf_op jit(solution)/shard_map/ppermute | solution.py:149
  61.0 2.0 collective-permute-start.8
  63.5 0.5 copy.67
  64.4 0.7 fusion.23
  65.1 0.6 fusion.1
  65.7 1.4 fusion.5
  67.1 5.7 %all-to-all-start.1 = ((bf16[16,32,128]{2,1,0:T(8,128)(2,1)}), bf16[16,32,128]{2,1,0:T(8,128)(2,1)S(1)}, u32[]{:S(2)}, u32[]{:S(2)}) async-start(bf16[16,32,128]{2,1,0:T(8,128)(2,1)} %bitcast.19), calls=%async_computation.1 | async-start | bytes 262144 | tf_op jit(solution)/shard_map/all_to_all | solution.py:142
  73.0 5.0 %all-to-all-done.1 = bf16[16,32,128]{2,1,0:T(8,128)(2,1)S(1)} async-done(((bf16[16,32,128]{2,1,0:T(8,128)(2,1)}), bf16[16,32,128]{2,1,0:T(8,128)(2,1)S(1)}, u32[]{:S(2)}, u32[]{:S(2)}) %all-to-all-start.1) | async-done | bytes 131104 | tf_op jit(solution)/shard_map/all_to_all | solution.py:142
  78.1 0.5 fusion.24
  78.6 2.1 %fusion.25 = f32[64,8,128]{2,0,1:T(8,128)S(1)} fusion(bf16[64,1024,1]{1,0,2:T(8,128)(2,1)S(1)} %reshape.620, bf16[8,1024,128]{2,1,0:T(8,128)(2,1)} %collective-permute-done.8), kind=kOutput, calls=%fused_computation.79 | convolution fusion | flops 134217728 | bytes 2490368 | tf_op jit(solution)/shard_map/tk,jkc->tjc/dot_general | solution.py:156
  80.8 0.4 copy.71
  81.2 0.4 reshape.614
  82.0 2.1 %convolution_convert_fusion.1 = bf16[512,2048]{1,0:T(8,128)(2,1)} fusion(pred[64,512]{1,0:T(8,128)(4,1)S(1)} %fusion.8, bf16[64,2048]{1,0:T(8,128)(2,1)S(1)} %fusion.11), kind=kOutput, calls=%fused_computation.6 | convolution fusion | flops 135266304 | bytes 2392064 | tf_op jit(solution)/shard_map/dot_general | solution.py:192
  84.1 7.1 %all-to-all-start.2 = ((bf16[16,32,2048]{2,1,0:T(8,128)(2,1)}), bf16[16,32,2048]{2,1,0:T(8,128)(2,1)}, u32[]{:S(2)}, u32[]{:S(2)}) async-start(bf16[16,32,2048]{2,1,0:T(8,128)(2,1)} %bitcast.25), calls=%async_computation.2 | async-start | bytes 4194304 | tf_op jit(solution)/shard_map/all_to_all | solution.py:195
  91.2 19.4 %collective-permute-done.10 = bf16[1,1024,1408]{2,1,0:T(8,128)(2,1)} collective-permute-done((bf16[1,1024,1408]{2,1,0:T(8,128)(2,1)}, bf16[1,1024,1408]{2,1,0:T(8,128)(2,1)}, u32[]{:S(2)}, u32[]{:S(2)}) %collective-permute-start.10) | collective-permute-done | bytes 2883616 | tf_op jit(solution)/shard_map/ppermute | solution.py:26
  110.6 8.7 %maximum_select_fusion = bf16[2048,1408]{1,0:T(8,128)(2,1)} fusion(bf16[1024,1408]{1,0:T(8,128)(2,1)} %bitcast.30, bf16[1024,1408]{1,0:T(8,128)(2,1)} %bitcast.29, pred[]{:T(512)S(6)} %eq.98), kind=kLoop, calls=%fused_computation | loop fusion | flops 25952256 | bytes 11534337 | tf_op jit(solution)/shard_map/jit(_where)/select_n | solution.py:201
  119.2 3.5 %maximum_select_fusion.1 = bf16[704,2048]{1,0:T(8,128)(2,1)S(1)} fusion(bf16[704,1024]{1,0:T(8,128)(2,1)} %bitcast.28, bf16[704,1024]{1,0:T(8,128)(2,1)} %bitcast.27, pred[]{:T(512)S(6)} %eq.98), kind=kLoop, calls=%fused_computation.7 | loop fusion | flops 12976128 | bytes 5767169 | tf_op jit(solution)/shard_map/jit(_where)/select_n | solution.py:206
  122.8 15.9 %all-to-all-done.2 = bf16[16,32,2048]{2,1,0:T(8,128)(2,1)} async-done(((bf16[16,32,2048]{2,1,0:T(8,128)(2,1)}), bf16[16,32,2048]{2,1,0:T(8,128)(2,1)}, u32[]{:S(2)}, u32[]{:S(2)}) %all-to-all-start.2) | async-done | bytes 2097184 | tf_op jit(solution)/shard_map/all_to_all | solution.py:195
  138.7 6.4 %fusion.26 = f32[512,1408]{1,0:T(8,128)S(1)} fusion(bf16[512,2048]{1,0:T(8,128)(2,1)} %bitcast.26, bf16[2048,1408]{1,0:T(8,128)(2,1)} %maximum_select_fusion), kind=kOutput, calls=%fused_computation.80 | convolution fusion | flops 2952790016 | bytes 10747904 | tf_op jit(solution)/shard_map/dot_general | solution.py:215
  145.1 3.3 %convolution_convert_fusion = bf16[512,2048]{1,0:T(8,128)(2,1)} fusion(bf16[704,2048]{1,0:T(8,128)(2,1)S(1)} %maximum_select_fusion.1, f32[512,1408]{1,0:T(8,128)S(1)} %fusion.26), kind=kOutput, calls=%fused_computation.5 | convolution fusion | flops 1479606272 | bytes 8126464 | tf_op jit(solution)/shard_map/dot_general | solution.py:217
  148.3 5.0 %all-to-all-start.3 = ((bf16[16,32,2048]{2,1,0:T(8,128)(2,1)}), bf16[16,32,2048]{2,1,0:T(8,128)(2,1)S(1)}, u32[]{:S(2)}, u32[]{:S(2)}) async-start(bf16[16,32,2048]{2,1,0:T(8,128)(2,1)} %bitcast.76), calls=%async_computation.3 | async-start | bytes 4194304 | tf_op jit(solution)/shard_map/all_to_all | solution.py:218
  153.5 47.2 %all-to-all-done.3 = bf16[16,32,2048]{2,1,0:T(8,128)(2,1)S(1)} async-done(((bf16[16,32,2048]{2,1,0:T(8,128)(2,1)}), bf16[16,32,2048]{2,1,0:T(8,128)(2,1)S(1)}, u32[]{:S(2)}, u32[]{:S(2)}) %all-to-all-start.3) | async-done | bytes 2097184 | tf_op jit(solution)/shard_map/all_to_all | solution.py:218
  200.8 1.9 fusion.2
  (61 shorter events, 3.4 us)
Async XLA Ops:
  0.0 7.9 %copy-start = (s32[2,96]{1,0:T(2,128)S(1)}, s32[2,96]{1,0:T(2,128)}, u32[]{:S(2)}) copy-start(s32[2,96]{1,0:T(2,128)} %param.15) | copy-start | bytes 2308
  0.0 27.4 %copy-start.1 = (bf16[512,128]{1,0:T(8,128)(2,1)S(1)}, bf16[512,128]{1,0:T(8,128)(2,1)}, u32[]{:S(2)}) copy-start(bf16[512,128]{1,0:T(8,128)(2,1)} %param.18) | copy-start | bytes 393220
  0.0 10.8 %collective-permute-start.6 = (bf16[512,128]{1,0:T(8,128)(2,1)}, bf16[512,128]{1,0:T(8,128)(2,1)S(1)}, u32[]{:S(2)}, u32[]{:S(2)}) collective-permute-start(bf16[512,128]{1,0:T(8,128)(2,1)} %param.18), channel_id=1, source_target_pairs={{0,28},{1,29},{2,30},{3,31},{4,24},{5,25},{6,26},{7,27},{8,20},{9,... | collective-permute-start | bytes 393224 | tf_op jit(solution)/shard_map/ppermute | solution.py:87
  2.3 10.7 %collective-permute-start = (bf16[512,128]{1,0:T(8,128)(2,1)}, bf16[512,128]{1,0:T(8,128)(2,1)S(1)}, u32[]{:S(2)}, u32[]{:S(2)}) collective-permute-start(bf16[512,128]{1,0:T(8,128)(2,1)} %param.18), channel_id=1, source_target_pairs={{0,16},{1,17},{2,18},{3,19},{4,20},{5,21},{6,22},{7,23},{8,24},{9,... | collective-permute-start | bytes 393224 | tf_op jit(solution)/shard_map/ppermute | solution.py:87
  2.5 12.5 %collective-permute-start.1 = (bf16[512,128]{1,0:T(8,128)(2,1)}, bf16[512,128]{1,0:T(8,128)(2,1)S(1)}, u32[]{:S(2)}, u32[]{:S(2)}) collective-permute-start(bf16[512,128]{1,0:T(8,128)(2,1)} %param.18), channel_id=1, source_target_pairs={{0,4},{1,5},{2,6},{3,7},{4,0},{5,1},{6,2},{7,3},{8,12},{9,13},{10,... | collective-permute-start | bytes 393224 | tf_op jit(solution)/shard_map/ppermute | solution.py:85
  4.7 11.4 %collective-permute-start.2 = (bf16[512,128]{1,0:T(8,128)(2,1)}, bf16[512,128]{1,0:T(8,128)(2,1)S(1)}, u32[]{:S(2)}, u32[]{:S(2)}) collective-permute-start(bf16[512,128]{1,0:T(8,128)(2,1)} %param.18), channel_id=1, source_target_pairs={{0,20},{1,21},{2,22},{3,23},{4,16},{5,17},{6,18},{7,19},{8,28},{9,... | collective-permute-start | bytes 393224 | tf_op jit(solution)/shard_map/ppermute | solution.py:87
  5.6 10.8 %collective-permute-start.3 = (bf16[512,128]{1,0:T(8,128)(2,1)}, bf16[512,128]{1,0:T(8,128)(2,1)S(1)}, u32[]{:S(2)}, u32[]{:S(2)}) collective-permute-start(bf16[512,128]{1,0:T(8,128)(2,1)} %param.18), channel_id=1, source_target_pairs={{0,8},{1,9},{2,10},{3,11},{4,12},{5,13},{6,14},{7,15},{8,0},{9,1},... | collective-permute-start | bytes 393224 | tf_op jit(solution)/shard_map/ppermute | solution.py:85
  10.8 13.0 %collective-permute-start.4 = (bf16[512,128]{1,0:T(8,128)(2,1)}, bf16[512,128]{1,0:T(8,128)(2,1)S(1)}, u32[]{:S(2)}, u32[]{:S(2)}) collective-permute-start(bf16[512,128]{1,0:T(8,128)(2,1)} %param.18), channel_id=1, source_target_pairs={{0,24},{1,25},{2,26},{3,27},{4,28},{5,29},{6,30},{7,31},{8,16},{9,... | collective-permute-start | bytes 393224 | tf_op jit(solution)/shard_map/ppermute | solution.py:87
  13.0 14.5 %collective-permute-start.5 = (bf16[512,128]{1,0:T(8,128)(2,1)}, bf16[512,128]{1,0:T(8,128)(2,1)S(1)}, u32[]{:S(2)}, u32[]{:S(2)}) collective-permute-start(bf16[512,128]{1,0:T(8,128)(2,1)} %param.18), channel_id=1, source_target_pairs={{0,12},{1,13},{2,14},{3,15},{4,8},{5,9},{6,10},{7,11},{8,4},{9,5},... | collective-permute-start | bytes 393224 | tf_op jit(solution)/shard_map/ppermute | solution.py:85
  15.0 67.0 %collective-permute-start.9 = (bf16[1,704,1024]{2,1,0:T(8,128)(2,1)}, bf16[1,704,1024]{2,1,0:T(8,128)(2,1)}, u32[]{:S(2)}, u32[]{:S(2)}) collective-permute-start(bf16[1,704,1024]{2,1,0:T(8,128)(2,1)} %param.23), channel_id=1, source_target_pairs={{0,16},{16,0},{1,17},{17,1},{2,18},{18,2},{3,19},{19,3},{4,20},{20... | collective-permute-start | bytes 4325384 | tf_op jit(solution)/shard_map/ppermute | solution.py:26
  16.1 94.5 %collective-permute-start.10 = (bf16[1,1024,1408]{2,1,0:T(8,128)(2,1)}, bf16[1,1024,1408]{2,1,0:T(8,128)(2,1)}, u32[]{:S(2)}, u32[]{:S(2)}) collective-permute-start(bf16[1,1024,1408]{2,1,0:T(8,128)(2,1)} %param.22), channel_id=1, source_target_pairs={{0,16},{16,0},{1,17},{17,1},{2,18},{18,2},{3,19},{19,3},{4,20},{20... | collective-permute-start | bytes 8650760 | tf_op jit(solution)/shard_map/ppermute | solution.py:26
  27.7 1.5 copy-start.6
  28.3 7.6 %copy-start.7 = (s32[1,16]{1,0:T(1,128)S(1)}, s32[1,16]{1,0:T(1,128)}, u32[]{:S(2)}) copy-start(s32[1,16]{1,0:T(1,128)} %param.17) | copy-start | bytes 196
  28.8 31.9 %collective-permute-start.7 = (bf16[4,1024,128]{2,1,0:T(8,128)(2,1)S(1)}, bf16[4,1024,128]{2,1,0:T(8,128)(2,1)S(1)}, u32[]{:S(2)}, u32[]{:S(2)}) collective-permute-start(bf16[4,1024,128]{2,1,0:T(8,128)(2,1)S(1)} %pad_maximum_fusion.1), channel_id=1, source_target_pairs={{0,2},{1,3},{2,0},{3,1},{4,6},{5,7},{6,4},{7,5},{8,10},{9,11},{10,... | collective-permute-start | bytes 3145736 | tf_op jit(solution)/shard_map/ppermute | solution.py:149
  29.9 33.5 %all-to-all-start = ((bf16[16,224,128]{2,1,0:T(8,128)(2,1)}), bf16[16,224,128]{2,1,0:T(8,128)(2,1)S(1)}, u32[]{:S(2)}, u32[]{:S(2)}) async-start(bf16[16,224,128]{2,1,0:T(8,128)(2,1)} %pad_maximum_fusion.2), calls=%async_computation | async-start | bytes 1835008 | tf_op jit(solution)/shard_map/all_to_all | solution.py:124
  61.0 17.6 %collective-permute-start.8 = (bf16[8,1024,128]{2,1,0:T(8,128)(2,1)S(1)}, bf16[8,1024,128]{2,1,0:T(8,128)(2,1)}, u32[]{:S(2)}, u32[]{:S(2)}) collective-permute-start(bf16[8,1024,128]{2,1,0:T(8,128)(2,1)S(1)} %pad_maximum_fusion), channel_id=1, source_target_pairs={{0,1},{1,0},{2,3},{3,2},{4,5},{5,4},{6,7},{7,6},{8,9},{9,8},{10,11... | collective-permute-start | bytes 6291464 | tf_op jit(solution)/shard_map/ppermute | solution.py:154
  65.7 7.1 %copy-start.3 = (s32[64,6]{0,1:T(8,128)S(1)}, s32[64,6]{0,1:T(8,128)}, u32[]{:S(2)}) copy-start(s32[64,6]{0,1:T(8,128)} %param.20) | copy-start | bytes 4612
  67.1 10.9 %all-to-all-start.1 = ((bf16[16,32,128]{2,1,0:T(8,128)(2,1)}), bf16[16,32,128]{2,1,0:T(8,128)(2,1)S(1)}, u32[]{:S(2)}, u32[]{:S(2)}) async-start(bf16[16,32,128]{2,1,0:T(8,128)(2,1)} %bitcast.19), calls=%async_computation.1 | async-start | bytes 262144 | tf_op jit(solution)/shard_map/all_to_all | solution.py:142
  78.6 3.0 %copy-start.2 = (bf16[64,2048]{1,0:T(8,128)(2,1)S(1)}, bf16[64,2048]{1,0:T(8,128)(2,1)}, u32[]{:S(2)}) copy-start(bf16[64,2048]{1,0:T(8,128)(2,1)} %param.13) | copy-start | bytes 786436
  78.6 3.2 %copy-start.4 = (f32[2048]{0:T(1024)S(1)}, f32[2048]{0:T(1024)}, u32[]{:S(2)}) copy-start(f32[2048]{0:T(1024)} %param.19) | copy-start | bytes 24580
  84.1 54.6 %all-to-all-start.2 = ((bf16[16,32,2048]{2,1,0:T(8,128)(2,1)}), bf16[16,32,2048]{2,1,0:T(8,128)(2,1)}, u32[]{:S(2)}, u32[]{:S(2)}) async-start(bf16[16,32,2048]{2,1,0:T(8,128)(2,1)} %bitcast.25), calls=%async_computation.2 | async-start | bytes 4194304 | tf_op jit(solution)/shard_map/all_to_all | solution.py:195
  148.3 5.0 %copy-start.5 = (f32[64,6]{0,1:T(8,128)S(1)}, f32[64,6]{0,1:T(8,128)}, u32[]{:S(2)}) copy-start(f32[64,6]{0,1:T(8,128)} %param.21) | copy-start | bytes 4612
  148.3 52.4 %all-to-all-start.3 = ((bf16[16,32,2048]{2,1,0:T(8,128)(2,1)}), bf16[16,32,2048]{2,1,0:T(8,128)(2,1)S(1)}, u32[]{:S(2)}, u32[]{:S(2)}) async-start(bf16[16,32,2048]{2,1,0:T(8,128)(2,1)} %bitcast.76), calls=%async_computation.3 | async-start | bytes 4194304 | tf_op jit(solution)/shard_map/all_to_all | solution.py:218
where the time goes:
time: 203 us
  waiting for transfers between devices  122 us (60%)
  starting transfers between devices  36.1 us (18%)
  matrix products  18.3 us (9%)
  other arithmetic  18 us (9%)
  local copies, waits for them, and re-layouts  7.32 us (4%)
    all_to_all x1, waiting for transfers between devices, on_device(): lax.all_to_all(outcome.reshape(n_mp, capacity, d_model), 'mp', split_axis...  47.2 us
    ppermute x1, waiting for transfers between devices, on_device(): pair = lax.ppermute(block, 'mp', [(m, m ^ 1 << b) for m in range(n_mp)])  23.9 us
    ppermute x2, waiting for transfers between devices, swap_dp(): return lax.ppermute(x, 'dp', [(0, 1), (1, 0)])  19.4 us
    all_to_all x1, waiting for transfers between devices, on_device(): lax.all_to_all(sending.reshape(n_mp, capacity, d_model), 'mp', split_axis...  15.9 us
    select_n x1, other arithmetic, on_device(): jnp.where(first, jnp.concatenate([experts_in[0], in_other[0]], axis=0), j...  8.66 us
    ppermute x4, waiting for transfers between devices, on_device(): lax.ppermute(out_weight, ('dp', 'mp'), [(d * n_mp + m, (1 - d) * n_mp + (...  7.35 us
    all_to_all x1, starting transfers between devices, on_device(): lax.all_to_all(sending.reshape(n_mp, capacity, d_model), 'mp', split_axis...  7.07 us
    dot_general x1, matrix products, on_device(): gate_vals = jnp.dot(flat_rows, gate_up, preferred_element_type=jnp.float32)  6.38 us
  transfers between devices with their start and end apart: 15, of which 7 were waited for; matrix products, arithmetic and copies ran while one was open for 16% of the time, Pallas kernels for 0%

commit v1 on v0

--- a/solution.py
+++ b/solution.py
@@ -192,9 +192,20 @@
     sending = lax.dot_general(
         dispatch, normed, (((0,), (0,)), ((), ())), preferred_element_type=jnp.float32
     ).astype(jnp.bfloat16)
-    received = lax.all_to_all(
-        sending.reshape(n_mp, capacity, d_model), "mp", split_axis=0, concat_axis=0, tiled=True
-    )
+    x_2 = sending.reshape(n_mp, capacity, d_model)
+    ways, here = (lax.axis_size("mp"), lax.axis_index("mp"))
+    width_2 = x_2.shape[0] // ways
+    shape = list(x_2.shape)
+    shape[0] = width_2
+    height = shape[0]
+    shape[0] = height * ways
+    full = jnp.zeros(shape, x_2.dtype)
+    for mask in range(ways):
+        part = lax.dynamic_slice_in_dim(x_2, (here ^ mask) * width_2, width_2, axis=0)
+        if mask:
+            part = lax.ppermute(part, "mp", [(d_2, d_2 ^ mask) for d_2 in range(ways)])
+        full = lax.dynamic_update_slice_in_dim(full, part, (here ^ mask) * height, axis=0)
+    received = full
     flat_rows = received.reshape(-1, d_model)
     if n_dp == 2:
         first = row_index == 0

time: 203 us -> 250 us (1.23)
  waiting for transfers between devices: 122 us -> 160 us
  starting transfers between devices: 36.1 us -> 46.5 us
  matrix products: 18.3 us -> 14 us
    ppermute x0 -> x15, waiting for transfers between devices: none -> 39.4 us  [on_device(): part = lax.ppermute(part, 'mp', [(d_2, d_2 ^ mask) for d_2 in range(ways)])]
    ppermute x0 -> x15, starting transfers between devices: none -> 17.2 us  [on_device(): part = lax.ppermute(part, 'mp', [(d_2, d_2 ^ mask) for d_2 in range(ways)])]
    all_to_all x1 -> x0, waiting for transfers between devices: 15.9 us -> none  [on_device(): lax.all_to_all(sending.reshape(n_mp, capacity, d_model), 'mp', split_axis...]
    ppermute x2, waiting for transfers between devices: 19.4 us -> 27.2 us  [swap_dp(): return lax.ppermute(x, 'dp', [(0, 1), (1, 0)])]
    ppermute x1, waiting for transfers between devices: 23.9 us -> 31.5 us  [on_device(): pair = lax.ppermute(block, 'mp', [(m, m ^ 1 << b) for m in range(n_mp)])]
    all_to_all x1 -> x0, starting transfers between devices: 7.07 us -> none  [on_device(): lax.all_to_all(sending.reshape(n_mp, capacity, d_model), 'mp', split_axis...]
    dot_general x1, matrix products: 6.38 us -> 3.42 us  [on_device(): gate_vals = jnp.dot(flat_rows, gate_up, preferred_element_type=jnp.float32)]
  transfers between devices with their start and end apart: 15 -> 29, of which waited for: 7 -> 15; matrix products, arithmetic and copies ran while one was open for 16% -> 13% of each run, Pallas kernels for 0% -> 0%
where the time goes in v1:
time: 250 us; the launch traced here: 249 us
  waiting for transfers between devices  160 us (64%)
  starting transfers between devices  46.5 us (19%)
  other arithmetic  19.1 us (8%)
  matrix products  14 us (6%)
  local copies, waits for them, and re-layouts  8.61 us (3%)
    all_to_all x1, waiting for transfers between devices, on_device(): lax.all_to_all(outcome.reshape(n_mp, capacity, d_model), 'mp', split_axis...  47.2 us
    ppermute x15, waiting for transfers between devices, on_device(): part = lax.ppermute(part, 'mp', [(d_2, d_2 ^ mask) for d_2 in range(ways)])  39.4 us
    ppermute x1, waiting for transfers between devices, on_device(): pair = lax.ppermute(block, 'mp', [(m, m ^ 1 << b) for m in range(n_mp)])  31.5 us
    ppermute x2, waiting for transfers between devices, swap_dp(): return lax.ppermute(x, 'dp', [(0, 1), (1, 0)])  27.2 us
    ppermute x15, starting transfers between devices, on_device(): part = lax.ppermute(part, 'mp', [(d_2, d_2 ^ mask) for d_2 in range(ways)])  17.2 us
    select_n x1, other arithmetic, on_device(): jnp.where(first, jnp.concatenate([experts_in[0], in_other[0]], axis=0), j...  8.75 us
    ppermute x4, waiting for transfers between devices, on_device(): lax.ppermute(out_weight, ('dp', 'mp'), [(d * n_mp + m, (1 - d) * n_mp + (...  6.53 us
    all_to_all x1, starting transfers between devices, on_device(): lax.all_to_all(kv_send, 'mp', split_axis=0, concat_axis=0, tiled=True)  6.28 us
  transfers between devices with their start and end apart: 29, of which 15 were waited for; matrix products, arithmetic and copies ran while one was open for 13% of the time, Pallas kernels for 0%

profile of v1, /device:TPU:11, one launch (start us, length us, event | category | flops | bytes accessed | tf_op | source)
XLA Modules:
  0.0 248.5 jit_solution(13510298858584634974)
XLA Ops:
  0.0 2.3 collective-permute-start.6
  2.5 2.2 collective-permute-start.1
  4.7 1.0 collective-permute-start.2
  5.9 1.2 dynamic_slice.55
  7.1 1.3 fusion.19
  8.5 0.8 copy.72
  9.7 1.2 reshape.608
  11.2 0.9 copy.77
  12.3 2.2 collective-permute-start.4
  15.5 1.0 pad_maximum_fusion.2
  16.5 1.1 collective-permute-start.9
  18.0 6.5 %collective-permute-done.4 = bf16[512,128]{1,0:T(8,128)(2,1)S(1)} collective-permute-done((bf16[512,128]{1,0:T(8,128)(2,1)S(1)}, bf16[512,128]{1,0:T(8,128)(2,1)S(1)}, u32[]{:S(2)}, u32[]{:S(2)}) %collective-permute-start.4) | collective-permute-done | bytes 131104 | tf_op jit(solution)/shard_map/ppermute | solution.py:87
  24.5 2.8 %collective-permute-done.5 = bf16[512,128]{1,0:T(8,128)(2,1)S(1)} collective-permute-done((bf16[512,128]{1,0:T(8,128)(2,1)S(1)}, bf16[512,128]{1,0:T(8,128)(2,1)S(1)}, u32[]{:S(2)}, u32[]{:S(2)}) %collective-permute-start.5) | collective-permute-done | bytes 131104 | tf_op jit(solution)/shard_map/ppermute | solution.py:85
  28.6 6.3 %all-to-all-start = ((bf16[16,224,128]{2,1,0:T(8,128)(2,1)}), bf16[16,224,128]{2,1,0:T(8,128)(2,1)S(1)}, u32[]{:S(2)}, u32[]{:S(2)}) async-start(bf16[16,224,128]{2,1,0:T(8,128)(2,1)} %pad_maximum_fusion.2), calls=%async_computation | async-start | bytes 1835008 | tf_op jit(solution)/shard_map/all_to_all | solution.py:124
  35.6 0.9 reduce-window.6
  37.0 31.5 %collective-permute-done.7 = bf16[4,1024,128]{2,1,0:T(8,128)(2,1)S(1)} collective-permute-done((bf16[4,1024,128]{2,1,0:T(8,128)(2,1)S(1)}, bf16[4,1024,128]{2,1,0:T(8,128)(2,1)S(1)}, u32[]{:S(2)}, u32[]{:S(2)}) %collective-permute-start.7) | collective-permute-done | bytes 1048608 | tf_op jit(solution)/shard_map/ppermute | solution.py:149
  68.9 0.8 collective-permute-start.8
  70.6 0.7 fusion.24
  72.0 1.4 fusion.5
  73.4 5.8 %all-to-all-start.1 = ((bf16[16,32,128]{2,1,0:T(8,128)(2,1)}), bf16[16,32,128]{2,1,0:T(8,128)(2,1)S(1)}, u32[]{:S(2)}, u32[]{:S(2)}) async-start(bf16[16,32,128]{2,1,0:T(8,128)(2,1)} %bitcast.19), calls=%async_computation.1 | async-start | bytes 262144 | tf_op jit(solution)/shard_map/all_to_all | solution.py:142
  79.3 5.0 %all-to-all-done.1 = bf16[16,32,128]{2,1,0:T(8,128)(2,1)S(1)} async-done(((bf16[16,32,128]{2,1,0:T(8,128)(2,1)}), bf16[16,32,128]{2,1,0:T(8,128)(2,1)S(1)}, u32[]{:S(2)}, u32[]{:S(2)}) %all-to-all-start.1) | async-done | bytes 131104 | tf_op jit(solution)/shard_map/all_to_all | solution.py:142
  84.9 27.2 %collective-permute-done.25 = bf16[1,1024,1408]{2,1,0:T(8,128)(2,1)} collective-permute-done((bf16[1,1024,1408]{2,1,0:T(8,128)(2,1)}, bf16[1,1024,1408]{2,1,0:T(8,128)(2,1)}, u32[]{:S(2)}, u32[]{:S(2)}) %collective-permute-start.25) | collective-permute-done | bytes 2883616 | tf_op jit(solution)/shard_map/ppermute | solution.py:26
  112.1 8.7 %maximum_select_fusion = bf16[2048,1408]{1,0:T(8,128)(2,1)} fusion(bf16[1024,1408]{1,0:T(8,128)(2,1)} %bitcast.30, bf16[1024,1408]{1,0:T(8,128)(2,1)} %bitcast.29, pred[]{:T(512)S(6)} %eq.98), kind=kLoop, calls=%fused_computation | loop fusion | flops 25952256 | bytes 11534337 | tf_op jit(solution)/shard_map/jit(_where)/select_n | solution.py:212
  120.9 2.1 fusion.26
  124.3 0.8 convolution_convert_fusion.1
  125.5 1.9 collective-permute-start.10
  127.7 1.4 collective-permute-start.12
  129.2 1.5 collective-permute-start.13
  131.0 3.9 %maximum_select_fusion.1 = bf16[704,2048]{1,0:T(8,128)(2,1)S(1)} fusion(bf16[704,1024]{1,0:T(8,128)(2,1)} %bitcast.28, bf16[704,1024]{1,0:T(8,128)(2,1)} %bitcast.27, pred[]{:T(512)S(6)} %eq.98), kind=kLoop, calls=%fused_computation.7 | loop fusion | flops 12976128 | bytes 5767169 | tf_op jit(solution)/shard_map/jit(_where)/select_n | solution.py:217
  134.9 1.5 collective-permute-start.15
  136.4 1.3 collective-permute-start.16
  137.8 3.4 %collective-permute-start.17 = (bf16[1,32,2048]{2,1,0:T(8,128)(2,1)S(1)}, bf16[1,32,2048]{2,1,0:T(8,128)(2,1)S(1)}, u32[]{:S(2)}, u32[]{:S(2)}) collective-permute-start(bf16[1,32,2048]{2,1,0:T(8,128)(2,1)S(1)} %get-tuple-element.28), channel_id=1, source_target_pairs={{0,8},{1,9},{2,10},{3,11},{4,12},{5,13},{6,14},{7,15},{8,0},{9,1},... | collective-permute-start | bytes 393224 | tf_op jit(solution)/shard_map/ppermute | solution.py:206
  141.4 2.7 %collective-permute-start.19 = (bf16[1,32,2048]{2,1,0:T(8,128)(2,1)S(1)}, bf16[1,32,2048]{2,1,0:T(8,128)(2,1)S(1)}, u32[]{:S(2)}, u32[]{:S(2)}) collective-permute-start(bf16[1,32,2048]{2,1,0:T(8,128)(2,1)S(1)} %get-tuple-element.26), channel_id=1, source_target_pairs={{0,10},{1,11},{2,8},{3,9},{4,14},{5,15},{6,12},{7,13},{8,2},{9,3},... | collective-permute-start | bytes 393224 | tf_op jit(solution)/shard_map/ppermute | solution.py:206
  144.1 1.4 collective-permute-start.20
  145.8 1.2 collective-permute-start.21
  147.0 11.1 %collective-permute-done.17 = bf16[1,32,2048]{2,1,0:T(8,128)(2,1)S(1)} collective-permute-done((bf16[1,32,2048]{2,1,0:T(8,128)(2,1)S(1)}, bf16[1,32,2048]{2,1,0:T(8,128)(2,1)S(1)}, u32[]{:S(2)}, u32[]{:S(2)}) %collective-permute-start.17) | collective-permute-done | bytes 131104 | tf_op jit(solution)/shard_map/ppermute | solution.py:206
  158.1 2.8 %collective-permute-done.18 = bf16[1,32,2048]{2,1,0:T(8,128)(2,1)S(1)} collective-permute-done((bf16[1,32,2048]{2,1,0:T(8,128)(2,1)S(1)}, bf16[1,32,2048]{2,1,0:T(8,128)(2,1)S(1)}, u32[]{:S(2)}, u32[]{:S(2)}) %collective-permute-start.18) | collective-permute-done | bytes 131104 | tf_op jit(solution)/shard_map/ppermute | solution.py:206
  161.0 8.2 %collective-permute-done.19 = bf16[1,32,2048]{2,1,0:T(8,128)(2,1)S(1)} collective-permute-done((bf16[1,32,2048]{2,1,0:T(8,128)(2,1)S(1)}, bf16[1,32,2048]{2,1,0:T(8,128)(2,1)S(1)}, u32[]{:S(2)}, u32[]{:S(2)}) %collective-permute-start.19) | collective-permute-done | bytes 131104 | tf_op jit(solution)/shard_map/ppermute | solution.py:206
  169.2 2.9 %collective-permute-done.20 = bf16[1,32,2048]{2,1,0:T(8,128)(2,1)S(1)} collective-permute-done((bf16[1,32,2048]{2,1,0:T(8,128)(2,1)S(1)}, bf16[1,32,2048]{2,1,0:T(8,128)(2,1)S(1)}, u32[]{:S(2)}, u32[]{:S(2)}) %collective-permute-start.20) | collective-permute-done | bytes 131104 | tf_op jit(solution)/shard_map/ppermute | solution.py:206
  172.2 2.8 %collective-permute-done.21 = bf16[1,32,2048]{2,1,0:T(8,128)(2,1)S(1)} collective-permute-done((bf16[1,32,2048]{2,1,0:T(8,128)(2,1)S(1)}, bf16[1,32,2048]{2,1,0:T(8,128)(2,1)S(1)}, u32[]{:S(2)}, u32[]{:S(2)}) %collective-permute-start.21) | collective-permute-done | bytes 131104 | tf_op jit(solution)/shard_map/ppermute | solution.py:206
  175.0 6.6 %collective-permute-done.22 = bf16[1,32,2048]{2,1,0:T(8,128)(2,1)S(1)} collective-permute-done((bf16[1,32,2048]{2,1,0:T(8,128)(2,1)S(1)}, bf16[1,32,2048]{2,1,0:T(8,128)(2,1)S(1)}, u32[]{:S(2)}, u32[]{:S(2)}) %collective-permute-start.22) | collective-permute-done | bytes 131104 | tf_op jit(solution)/shard_map/ppermute | solution.py:206
  181.6 1.9 collective-permute-done.23
  183.5 2.8 %collective-permute-done.24 = bf16[1,32,2048]{2,1,0:T(8,128)(2,1)S(1)} collective-permute-done((bf16[1,32,2048]{2,1,0:T(8,128)(2,1)S(1)}, bf16[1,32,2048]{2,1,0:T(8,128)(2,1)S(1)}, u32[]{:S(2)}, u32[]{:S(2)}) %collective-permute-start.24) | collective-permute-done | bytes 131104 | tf_op jit(solution)/shard_map/ppermute | solution.py:206
  186.3 3.4 %fusion.27 = f32[512,1408]{1,0:T(8,128)S(1)} fusion(bf16[512,2048]{1,0:T(8,128)(2,1)S(1)} %bitcast.79, bf16[2048,1408]{1,0:T(8,128)(2,1)S(1)} %bitcast.76), kind=kOutput, calls=%fused_computation.112 | convolution fusion | flops 2952790016 | bytes 10747904 | tf_op jit(solution)/shard_map/dot_general | solution.py:226
  189.8 3.2 %convolution_convert_fusion = bf16[512,2048]{1,0:T(8,128)(2,1)} fusion(bf16[704,2048]{1,0:T(8,128)(2,1)S(1)} %maximum_select_fusion.1, f32[512,1408]{1,0:T(8,128)S(1)} %fusion.27), kind=kOutput, calls=%fused_computation.5 | convolution fusion | flops 1479606272 | bytes 8126464 | tf_op jit(solution)/shard_map/dot_general | solution.py:228
  193.0 6.2 %all-to-all-start.2 = ((bf16[16,32,2048]{2,1,0:T(8,128)(2,1)}), bf16[16,32,2048]{2,1,0:T(8,128)(2,1)S(1)}, u32[]{:S(2)}, u32[]{:S(2)}) async-start(bf16[16,32,2048]{2,1,0:T(8,128)(2,1)} %bitcast.80), calls=%async_computation.2 | async-start | bytes 4194304 | tf_op jit(solution)/shard_map/all_to_all | solution.py:229
  199.4 47.2 %all-to-all-done.2 = bf16[16,32,2048]{2,1,0:T(8,128)(2,1)S(1)} async-done(((bf16[16,32,2048]{2,1,0:T(8,128)(2,1)}), bf16[16,32,2048]{2,1,0:T(8,128)(2,1)S(1)}, u32[]{:S(2)}, u32[]{:S(2)}) %all-to-all-start.2) | async-done | bytes 2097184 | tf_op jit(solution)/shard_map/all_to_all | solution.py:229
  246.6 1.9 fusion.2
  (107 shorter events, 10.8 us)
Async XLA Ops:
  0.0 8.5 %copy-start = (s32[2,96]{1,0:T(2,128)S(1)}, s32[2,96]{1,0:T(2,128)}, u32[]{:S(2)}) copy-start(s32[2,96]{1,0:T(2,128)} %param.15) | copy-start | bytes 2308
  0.0 12.3 %copy-start.1 = (bf16[512,128]{1,0:T(8,128)(2,1)S(1)}, bf16[512,128]{1,0:T(8,128)(2,1)}, u32[]{:S(2)}) copy-start(bf16[512,128]{1,0:T(8,128)(2,1)} %param.18) | copy-start | bytes 393220
  0.0 12.3 %collective-permute-start.6 = (bf16[512,128]{1,0:T(8,128)(2,1)}, bf16[512,128]{1,0:T(8,128)(2,1)S(1)}, u32[]{:S(2)}, u32[]{:S(2)}) collective-permute-start(bf16[512,128]{1,0:T(8,128)(2,1)} %param.18), channel_id=1, source_target_pairs={{0,28},{1,29},{2,30},{3,31},{4,24},{5,25},{6,26},{7,27},{8,20},{9,... | collective-permute-start | bytes 393224 | tf_op jit(solution)/shard_map/ppermute | solution.py:87
  2.3 12.3 %collective-permute-start = (bf16[512,128]{1,0:T(8,128)(2,1)}, bf16[512,128]{1,0:T(8,128)(2,1)S(1)}, u32[]{:S(2)}, u32[]{:S(2)}) collective-permute-start(bf16[512,128]{1,0:T(8,128)(2,1)} %param.18), channel_id=1, source_target_pairs={{0,16},{1,17},{2,18},{3,19},{4,20},{5,21},{6,22},{7,23},{8,24},{9,... | collective-permute-start | bytes 393224 | tf_op jit(solution)/shard_map/ppermute | solution.py:87
  2.5 14.0 %collective-permute-start.1 = (bf16[512,128]{1,0:T(8,128)(2,1)}, bf16[512,128]{1,0:T(8,128)(2,1)S(1)}, u32[]{:S(2)}, u32[]{:S(2)}) collective-permute-start(bf16[512,128]{1,0:T(8,128)(2,1)} %param.18), channel_id=1, source_target_pairs={{0,4},{1,5},{2,6},{3,7},{4,0},{5,1},{6,2},{7,3},{8,12},{9,13},{10,... | collective-permute-start | bytes 393224 | tf_op jit(solution)/shard_map/ppermute | solution.py:85
  4.7 12.9 %collective-permute-start.2 = (bf16[512,128]{1,0:T(8,128)(2,1)}, bf16[512,128]{1,0:T(8,128)(2,1)S(1)}, u32[]{:S(2)}, u32[]{:S(2)}) collective-permute-start(bf16[512,128]{1,0:T(8,128)(2,1)} %param.18), channel_id=1, source_target_pairs={{0,20},{1,21},{2,22},{3,23},{4,16},{5,17},{6,18},{7,19},{8,28},{9,... | collective-permute-start | bytes 393224 | tf_op jit(solution)/shard_map/ppermute | solution.py:87
  5.6 12.3 %collective-permute-start.3 = (bf16[512,128]{1,0:T(8,128)(2,1)}, bf16[512,128]{1,0:T(8,128)(2,1)S(1)}, u32[]{:S(2)}, u32[]{:S(2)}) collective-permute-start(bf16[512,128]{1,0:T(8,128)(2,1)} %param.18), channel_id=1, source_target_pairs={{0,8},{1,9},{2,10},{3,11},{4,12},{5,13},{6,14},{7,15},{8,0},{9,1},... | collective-permute-start | bytes 393224 | tf_op jit(solution)/shard_map/ppermute | solution.py:85
  12.3 12.2 %collective-permute-start.4 = (bf16[512,128]{1,0:T(8,128)(2,1)S(1)}, bf16[512,128]{1,0:T(8,128)(2,1)S(1)}, u32[]{:S(2)}, u32[]{:S(2)}) collective-permute-start(bf16[512,128]{1,0:T(8,128)(2,1)S(1)} %copy-done.1), channel_id=1, source_target_pairs={{0,24},{1,25},{2,26},{3,27},{4,28},{5,29},{6,30},{7,31},{8,16},{9,... | collective-permute-start | bytes 393224 | tf_op jit(solution)/shard_map/ppermute | solution.py:87
  14.5 12.8 %collective-permute-start.5 = (bf16[512,128]{1,0:T(8,128)(2,1)S(1)}, bf16[512,128]{1,0:T(8,128)(2,1)S(1)}, u32[]{:S(2)}, u32[]{:S(2)}) collective-permute-start(bf16[512,128]{1,0:T(8,128)(2,1)S(1)} %copy-done.1), channel_id=1, source_target_pairs={{0,12},{1,13},{2,14},{3,15},{4,8},{5,9},{6,10},{7,11},{8,4},{9,5},... | collective-permute-start | bytes 393224 | tf_op jit(solution)/shard_map/ppermute | solution.py:85
  16.5 107.8 %collective-permute-start.9 = (bf16[1,704,1024]{2,1,0:T(8,128)(2,1)}, bf16[1,704,1024]{2,1,0:T(8,128)(2,1)}, u32[]{:S(2)}, u32[]{:S(2)}) collective-permute-start(bf16[1,704,1024]{2,1,0:T(8,128)(2,1)} %param.23), channel_id=1, source_target_pairs={{0,16},{16,0},{1,17},{17,1},{2,18},{18,2},{3,19},{19,3},{4,20},{20... | collective-permute-start | bytes 4325384 | tf_op jit(solution)/shard_map/ppermute | solution.py:26
  17.6 94.5 %collective-permute-start.25 = (bf16[1,1024,1408]{2,1,0:T(8,128)(2,1)}, bf16[1,1024,1408]{2,1,0:T(8,128)(2,1)}, u32[]{:S(2)}, u32[]{:S(2)}) collective-permute-start(bf16[1,1024,1408]{2,1,0:T(8,128)(2,1)} %param.22), channel_id=1, source_target_pairs={{0,16},{16,0},{1,17},{17,1},{2,18},{18,2},{3,19},{19,3},{4,20},{20... | collective-permute-start | bytes 8650760 | tf_op jit(solution)/shard_map/ppermute | solution.py:26
  28.6 41.1 %all-to-all-start = ((bf16[16,224,128]{2,1,0:T(8,128)(2,1)}), bf16[16,224,128]{2,1,0:T(8,128)(2,1)S(1)}, u32[]{:S(2)}, u32[]{:S(2)}) async-start(bf16[16,224,128]{2,1,0:T(8,128)(2,1)} %pad_maximum_fusion.2), calls=%async_computation | async-start | bytes 1835008 | tf_op jit(solution)/shard_map/all_to_all | solution.py:124
  35.0 33.5 %collective-permute-start.7 = (bf16[4,1024,128]{2,1,0:T(8,128)(2,1)S(1)}, bf16[4,1024,128]{2,1,0:T(8,128)(2,1)S(1)}, u32[]{:S(2)}, u32[]{:S(2)}) collective-permute-start(bf16[4,1024,128]{2,1,0:T(8,128)(2,1)S(1)} %pad_maximum_fusion.1), channel_id=1, source_target_pairs={{0,2},{1,3},{2,0},{3,1},{4,6},{5,7},{6,4},{7,5},{8,10},{9,11},{10,... | collective-permute-start | bytes 3145736 | tf_op jit(solution)/shard_map/ppermute | solution.py:149
  68.9 52.0 %collective-permute-start.8 = (bf16[8,1024,128]{2,1,0:T(8,128)(2,1)S(1)}, bf16[8,1024,128]{2,1,0:T(8,128)(2,1)}, u32[]{:S(2)}, u32[]{:S(2)}) collective-permute-start(bf16[8,1024,128]{2,1,0:T(8,128)(2,1)S(1)} %pad_maximum_fusion), channel_id=1, source_target_pairs={{0,1},{1,0},{2,3},{3,2},{4,5},{5,4},{6,7},{7,6},{8,9},{9,8},{10,11... | collective-permute-start | bytes 6291464 | tf_op jit(solution)/shard_map/ppermute | solution.py:154
  72.0 7.2 %copy-start.3 = (s32[64,6]{0,1:T(8,128)S(1)}, s32[64,6]{0,1:T(8,128)}, u32[]{:S(2)}) copy-start(s32[64,6]{0,1:T(8,128)} %param.20) | copy-start | bytes 4612
  73.4 10.9 %all-to-all-start.1 = ((bf16[16,32,128]{2,1,0:T(8,128)(2,1)}), bf16[16,32,128]{2,1,0:T(8,128)(2,1)S(1)}, u32[]{:S(2)}, u32[]{:S(2)}) async-start(bf16[16,32,128]{2,1,0:T(8,128)(2,1)} %bitcast.19), calls=%async_computation.1 | async-start | bytes 262144 | tf_op jit(solution)/shard_map/all_to_all | solution.py:142
  123.0 1.0 copy-start.2
  123.0 1.1 copy-start.4
  125.3 61.1 %slice-start = ((s8[5767168]{0:T(1024)(128)(4,1)}), s8[4194304]{0:T(1024)(128)(4,1)S(1)}, s32[]{:S(2)}) async-start(s8[5767168]{0:T(1024)(128)(4,1)} %bitcast.75), calls=%async_computation.3 | async-start | bytes 8388608
  125.5 9.4 %collective-permute-start.10 = (bf16[1,32,2048]{2,1,0:T(8,128)(2,1)S(1)}, bf16[1,32,2048]{2,1,0:T(8,128)(2,1)S(1)}, u32[]{:S(2)}, u32[]{:S(2)}) collective-permute-start(bf16[1,32,2048]{2,1,0:T(8,128)(2,1)S(1)} %get-tuple-element.35), channel_id=1, source_target_pairs={{0,1},{1,0},{2,3},{3,2},{4,5},{5,4},{6,7},{7,6},{8,9},{9,8},{10,11... | collective-permute-start | bytes 393224 | tf_op jit(solution)/shard_map/ppermute | solution.py:206
  127.5 9.0 %collective-permute-start.11 = (bf16[1,32,2048]{2,1,0:T(8,128)(2,1)S(1)}, bf16[1,32,2048]{2,1,0:T(8,128)(2,1)S(1)}, u32[]{:S(2)}, u32[]{:S(2)}) collective-permute-start(bf16[1,32,2048]{2,1,0:T(8,128)(2,1)S(1)} %get-tuple-element.34), channel_id=1, source_target_pairs={{0,2},{1,3},{2,0},{3,1},{4,6},{5,7},{6,4},{7,5},{8,10},{9,11},{10,... | collective-permute-start | bytes 393224 | tf_op jit(solution)/shard_map/ppermute | solution.py:206
  127.7 10.0 %collective-permute-start.12 = (bf16[1,32,2048]{2,1,0:T(8,128)(2,1)S(1)}, bf16[1,32,2048]{2,1,0:T(8,128)(2,1)S(1)}, u32[]{:S(2)}, u32[]{:S(2)}) collective-permute-start(bf16[1,32,2048]{2,1,0:T(8,128)(2,1)S(1)} %get-tuple-element.33), channel_id=1, source_target_pairs={{0,3},{1,2},{2,1},{3,0},{4,7},{5,6},{6,5},{7,4},{8,11},{9,10},{10,... | collective-permute-start | bytes 393224 | tf_op jit(solution)/shard_map/ppermute | solution.py:206
  129.2 12.0 %collective-permute-start.13 = (bf16[1,32,2048]{2,1,0:T(8,128)(2,1)S(1)}, bf16[1,32,2048]{2,1,0:T(8,128)(2,1)S(1)}, u32[]{:S(2)}, u32[]{:S(2)}) collective-permute-start(bf16[1,32,2048]{2,1,0:T(8,128)(2,1)S(1)} %get-tuple-element.32), channel_id=1, source_target_pairs={{0,4},{1,5},{2,6},{3,7},{4,0},{5,1},{6,2},{7,3},{8,12},{9,13},{10,... | collective-permute-start | bytes 393224 | tf_op jit(solution)/shard_map/ppermute | solution.py:206
  130.6 10.8 %collective-permute-start.14 = (bf16[1,32,2048]{2,1,0:T(8,128)(2,1)S(1)}, bf16[1,32,2048]{2,1,0:T(8,128)(2,1)S(1)}, u32[]{:S(2)}, u32[]{:S(2)}) collective-permute-start(bf16[1,32,2048]{2,1,0:T(8,128)(2,1)S(1)} %get-tuple-element.31), channel_id=1, source_target_pairs={{0,5},{1,4},{2,7},{3,6},{4,1},{5,0},{6,3},{7,2},{8,13},{9,12},{10,... | collective-permute-start | bytes 393224 | tf_op jit(solution)/shard_map/ppermute | solution.py:206
  131.0 55.4 %slice-start.1 = ((s8[5767168]{0:T(1024)(128)(4,1)}), s8[1572864]{0:T(1024)(128)(4,1)S(1)}, s32[]{:S(2)}) async-start(s8[5767168]{0:T(1024)(128)(4,1)} %bitcast.75), calls=%async_computation.4 | async-start | bytes 3145728
  134.9 9.2 %collective-permute-start.15 = (bf16[1,32,2048]{2,1,0:T(8,128)(2,1)S(1)}, bf16[1,32,2048]{2,1,0:T(8,128)(2,1)S(1)}, u32[]{:S(2)}, u32[]{:S(2)}) collective-permute-start(bf16[1,32,2048]{2,1,0:T(8,128)(2,1)S(1)} %get-tuple-element.30), channel_id=1, source_target_pairs={{0,6},{1,7},{2,4},{3,5},{4,2},{5,3},{6,0},{7,1},{8,14},{9,15},{10,... | collective-permute-start | bytes 393224 | tf_op jit(solution)/shard_map/ppermute | solution.py:206
  136.4 9.4 %collective-permute-start.16 = (bf16[1,32,2048]{2,1,0:T(8,128)(2,1)S(1)}, bf16[1,32,2048]{2,1,0:T(8,128)(2,1)S(1)}, u32[]{:S(2)}, u32[]{:S(2)}) collective-permute-start(bf16[1,32,2048]{2,1,0:T(8,128)(2,1)S(1)} %get-tuple-element.29), channel_id=1, source_target_pairs={{0,7},{1,6},{2,5},{3,4},{4,3},{5,2},{6,1},{7,0},{8,15},{9,14},{10,... | collective-permute-start | bytes 393224 | tf_op jit(solution)/shard_map/ppermute | solution.py:206
  137.8 20.3 %collective-permute-start.17 = (bf16[1,32,2048]{2,1,0:T(8,128)(2,1)S(1)}, bf16[1,32,2048]{2,1,0:T(8,128)(2,1)S(1)}, u32[]{:S(2)}, u32[]{:S(2)}) collective-permute-start(bf16[1,32,2048]{2,1,0:T(8,128)(2,1)S(1)} %get-tuple-element.28), channel_id=1, source_target_pairs={{0,8},{1,9},{2,10},{3,11},{4,12},{5,13},{6,14},{7,15},{8,0},{9,1},... | collective-permute-start | bytes 393224 | tf_op jit(solution)/shard_map/ppermute | solution.py:206
  141.2 19.7 %collective-permute-start.18 = (bf16[1,32,2048]{2,1,0:T(8,128)(2,1)S(1)}, bf16[1,32,2048]{2,1,0:T(8,128)(2,1)S(1)}, u32[]{:S(2)}, u32[]{:S(2)}) collective-permute-start(bf16[1,32,2048]{2,1,0:T(8,128)(2,1)S(1)} %get-tuple-element.27), channel_id=1, source_target_pairs={{0,9},{1,8},{2,11},{3,10},{4,13},{5,12},{6,15},{7,14},{8,1},{9,0},... | collective-permute-start | bytes 393224 | tf_op jit(solution)/shard_map/ppermute | solution.py:206
  141.4 27.8 %collective-permute-start.19 = (bf16[1,32,2048]{2,1,0:T(8,128)(2,1)S(1)}, bf16[1,32,2048]{2,1,0:T(8,128)(2,1)S(1)}, u32[]{:S(2)}, u32[]{:S(2)}) collective-permute-start(bf16[1,32,2048]{2,1,0:T(8,128)(2,1)S(1)} %get-tuple-element.26), channel_id=1, source_target_pairs={{0,10},{1,11},{2,8},{3,9},{4,14},{5,15},{6,12},{7,13},{8,2},{9,3},... | collective-permute-start | bytes 393224 | tf_op jit(solution)/shard_map/ppermute | solution.py:206
  144.1 28.1 %collective-permute-start.20 = (bf16[1,32,2048]{2,1,0:T(8,128)(2,1)S(1)}, bf16[1,32,2048]{2,1,0:T(8,128)(2,1)S(1)}, u32[]{:S(2)}, u32[]{:S(2)}) collective-permute-start(bf16[1,32,2048]{2,1,0:T(8,128)(2,1)S(1)} %get-tuple-element.25), channel_id=1, source_target_pairs={{0,11},{1,10},{2,9},{3,8},{4,15},{5,14},{6,13},{7,12},{8,3},{9,2},... | collective-permute-start | bytes 393224 | tf_op jit(solution)/shard_map/ppermute | solution.py:206
  145.8 29.1 %collective-permute-start.21 = (bf16[1,32,2048]{2,1,0:T(8,128)(2,1)S(1)}, bf16[1,32,2048]{2,1,0:T(8,128)(2,1)S(1)}, u32[]{:S(2)}, u32[]{:S(2)}) collective-permute-start(bf16[1,32,2048]{2,1,0:T(8,128)(2,1)S(1)} %get-tuple-element.24), channel_id=1, source_target_pairs={{0,12},{1,13},{2,14},{3,15},{4,8},{5,9},{6,10},{7,11},{8,4},{9,5},... | collective-permute-start | bytes 393224 | tf_op jit(solution)/shard_map/ppermute | solution.py:206
  158.1 23.5 %collective-permute-start.22 = (bf16[1,32,2048]{2,1,0:T(8,128)(2,1)S(1)}, bf16[1,32,2048]{2,1,0:T(8,128)(2,1)S(1)}, u32[]{:S(2)}, u32[]{:S(2)}) collective-permute-start(bf16[1,32,2048]{2,1,0:T(8,128)(2,1)S(1)} %get-tuple-element.23), channel_id=1, source_target_pairs={{0,13},{1,12},{2,15},{3,14},{4,9},{5,8},{6,11},{7,10},{8,5},{9,4},... | collective-permute-start | bytes 393224 | tf_op jit(solution)/shard_map/ppermute | solution.py:206
  160.9 22.6 %collective-permute-start.23 = (bf16[1,32,2048]{2,1,0:T(8,128)(2,1)S(1)}, bf16[1,32,2048]{2,1,0:T(8,128)(2,1)S(1)}, u32[]{:S(2)}, u32[]{:S(2)}) collective-permute-start(bf16[1,32,2048]{2,1,0:T(8,128)(2,1)S(1)} %get-tuple-element.22), channel_id=1, source_target_pairs={{0,14},{1,15},{2,12},{3,13},{4,10},{5,11},{6,8},{7,9},{8,6},{9,7},... | collective-permute-start | bytes 393224 | tf_op jit(solution)/shard_map/ppermute | solution.py:206
  169.2 17.1 %collective-permute-start.24 = (bf16[1,32,2048]{2,1,0:T(8,128)(2,1)S(1)}, bf16[1,32,2048]{2,1,0:T(8,128)(2,1)S(1)}, u32[]{:S(2)}, u32[]{:S(2)}) collective-permute-start(bf16[1,32,2048]{2,1,0:T(8,128)(2,1)S(1)} %get-tuple-element.21), channel_id=1, source_target_pairs={{0,15},{1,14},{2,13},{3,12},{4,11},{5,10},{6,9},{7,8},{8,7},{9,6},... | collective-permute-start | bytes 393224 | tf_op jit(solution)/shard_map/ppermute | solution.py:206
  193.0 6.2 %copy-start.5 = (f32[64,6]{0,1:T(8,128)S(1)}, f32[64,6]{0,1:T(8,128)}, u32[]{:S(2)}) copy-start(f32[64,6]{0,1:T(8,128)} %param.21) | copy-start | bytes 4612
  193.0 53.6 %all-to-all-start.2 = ((bf16[16,32,2048]{2,1,0:T(8,128)(2,1)}), bf16[16,32,2048]{2,1,0:T(8,128)(2,1)S(1)}, u32[]{:S(2)}, u32[]{:S(2)}) async-start(bf16[16,32,2048]{2,1,0:T(8,128)(2,1)} %bitcast.80), calls=%async_computation.2 | async-start | bytes 4194304 | tf_op jit(solution)/shard_map/all_to_all | solution.py:229
